TPU v7x, 32 devices: a whole 2x2x4 slice. The times are simulated.
32 devices in a mesh: seq: 8 (over y, x, core), fsdp: 4 (over z).
Axes of the slice: x: 2, y: 2, z: 4, core: 2. Of those that a mesh axis runs over, the one named last changes fastest.
Arguments:
- query_states: bfloat16 [2048, 4096], P('seq', 'fsdp'), may hold values from -24 to 24
- key_states: bfloat16 [2048, 4096], P('seq', 'fsdp'), may hold values from -6 to 6
- value_states: bfloat16 [2048, 4096], P('seq', 'fsdp'), may hold values from -6 to 6
- positions: int32 [2048], P('seq'), may hold values from 0 to 2047, as said below
- out_weight: bfloat16 [4096, 5120], P('fsdp', 'seq'), may hold values from -1 to 1
- cotangent: bfloat16 [2048, 5120], P('seq', 'fsdp'), may hold values from -0.59765625 to 0.59765625
Outputs:
- attn_output: float32 [2048, 5120], P('seq', 'fsdp')
- grad_queries: float32 [2048, 4096], P('seq', 'fsdp')
- grad_keys: float32 [2048, 4096], P('seq', 'fsdp')
- grad_values: float32 [2048, 4096], P('seq', 'fsdp')
- grad_weight: float32 [4096, 5120], P('fsdp', 'seq')
Inputs may be any that keep to these rules, and one draw needn't show every extreme that they name: A permutation of 0 to 2047; each aligned block of 256 rows holds, in increasing order, the positions of one residue class modulo 2048 // 256.
All inputs are finite; a program needn't handle non-finite values.
Results may differ from a plain program's by a relative error of at most 0.02.
Values may be sent and summed in bfloat16 or wider, within the bound.
No kernel may reach another device: no remote copies, remote signals or barrier semaphores. Data moves between devices by JAX's collectives and lax.ppermute only.
A program may use at most 128 MiB of HBM per device.

v0:
```python
import jax
import jax.numpy as jnp
from jax import lax
from jax.sharding import PartitionSpec as P

HEAD_DIM = 128
blocked = -1e30


def shifted(block, axis, distance):
    devices = range(lax.axis_size(axis))
    route = [((i - distance) % len(devices), i) for i in devices]
    return lax.ppermute(block, axis, route)


def split_heads(matrix):
    return matrix.reshape(matrix.shape[0], -1, HEAD_DIM)


def masked_scores(query_rows, key_rows, query_pos, key_pos):
    raw = jnp.einsum(
        "qhd,khd->hqk", query_rows, key_rows, preferred_element_type=jnp.float32
    ) * HEAD_DIM ** (-0.5)
    visible = key_pos[None, None, :] <= query_pos[None, :, None]
    return jnp.where(visible, raw, blocked)


def tile_grads(
    query_rows, grad_rows, log_total, row_delta, query_pos, key_rows, value_rows, key_pos
):
    scores = masked_scores(query_rows, key_rows, query_pos, key_pos)
    probs = jnp.exp(scores - log_total[:, :, None])
    grad_probs = jnp.einsum(
        "qhd,khd->hqk", grad_rows, value_rows, preferred_element_type=jnp.float32
    )
    grad_scores = (probs * (grad_probs - row_delta[:, :, None])).astype(jnp.bfloat16)
    grad_query = jnp.einsum(
        "hqk,khd->qhd", grad_scores, key_rows, preferred_element_type=jnp.float32
    )
    grad_key = jnp.einsum(
        "hqk,qhd->khd", grad_scores, query_rows, preferred_element_type=jnp.float32
    )
    grad_value = jnp.einsum(
        "hqk,qhd->khd", probs.astype(jnp.bfloat16), grad_rows, preferred_element_type=jnp.float32
    )
    return (grad_query, grad_key, grad_value)


def shards(query_states, key_states, value_states, positions, out_weight, cotangent):
    local_tokens = query_states.shape[0]
    query_heads = split_heads(query_states)
    key_heads = split_heads(key_states)
    value_heads = split_heads(value_states)
    local_heads = query_heads.shape[1]
    row_max = jnp.full((local_heads, local_tokens), blocked, jnp.float32)
    piece_keys = lax.all_gather(key_states, "seq", axis=0, tiled=True)
    piece_pos = lax.all_gather(positions, "seq", axis=0, tiled=True)
    scores = masked_scores(query_heads, split_heads(piece_keys), positions, piece_pos)
    new_max = jnp.maximum(row_max, jnp.max(scores, axis=2))
    new_total = jnp.sum(jnp.exp(scores - new_max[:, :, None]), axis=2)
    log_total = new_max + jnp.log(new_total)
    zero_heads = jnp.zeros((local_tokens, local_heads, HEAD_DIM), jnp.float32)
    piece_keys = lax.all_gather(key_states, "seq", axis=0, tiled=True)
    piece_values = lax.all_gather(value_states, "seq", axis=0, tiled=True)
    piece_pos = lax.all_gather(positions, "seq", axis=0, tiled=True)
    scores = masked_scores(query_heads, split_heads(piece_keys), positions, piece_pos)
    weights = jnp.exp(scores - log_total[:, :, None]).astype(jnp.bfloat16)
    attended = jnp.einsum(
        "hqk,khd->qhd", weights, split_heads(piece_values), preferred_element_type=jnp.float32
    )
    attended_heads = attended.astype(jnp.bfloat16)
    attended_flat = attended_heads.reshape(local_tokens, local_heads * HEAD_DIM)
    weight_full = lax.all_gather(out_weight, "seq", axis=1, tiled=True)
    partial_sum = jnp.dot(attended_flat, weight_full, preferred_element_type=jnp.float32).astype(
        jnp.bfloat16
    )
    attn_output = lax.psum_scatter(partial_sum, "fsdp", scatter_dimension=1, tiled=True).astype(
        jnp.float32
    )
    cotangent_full = lax.all_gather(cotangent, "fsdp", axis=1, tiled=True)
    grad_attended = jnp.einsum(
        "td,hd->th", cotangent_full, weight_full, preferred_element_type=jnp.float32
    ).astype(jnp.bfloat16)
    weight_term = jnp.einsum(
        "th,td->hd", attended_flat, cotangent_full, preferred_element_type=jnp.float32
    )
    grad_weight = lax.psum_scatter(weight_term, "seq", scatter_dimension=1, tiled=True)
    grad_heads = split_heads(grad_attended)
    row_delta = jnp.sum(
        grad_heads.astype(jnp.float32) * attended_heads.astype(jnp.float32), axis=2
    ).T
    cycle_length = lax.axis_size("seq")

    def key_step(cycle_step, state_tuple):
        key_block, value_block, key_pos, key_grad, value_grad, query_grad = state_tuple
        grad_query, grad_key, grad_value = tile_grads(
            query_heads,
            grad_heads,
            log_total,
            row_delta,
            positions,
            key_block,
            value_block,
            key_pos,
        )
        key_block, value_block, key_pos = shifted((key_block, value_block, key_pos), "seq", 1)
        key_grad, value_grad = shifted((key_grad + grad_key, value_grad + grad_value), "seq", 1)
        return (key_block, value_block, key_pos, key_grad, value_grad, query_grad + grad_query)

    final_state = lax.fori_loop(
        0,
        cycle_length,
        key_step,
        (key_heads, value_heads, positions, zero_heads, zero_heads, zero_heads),
    )
    query_sum, key_sum, value_sum = (final_state[5], final_state[3], final_state[4])
    score_scale = HEAD_DIM ** (-0.5)
    grad_queries = (query_sum * score_scale).reshape(local_tokens, local_heads * HEAD_DIM)
    grad_keys = (key_sum * score_scale).reshape(local_tokens, local_heads * HEAD_DIM)
    grad_values = value_sum.reshape(local_tokens, local_heads * HEAD_DIM)
    return (attn_output, grad_queries, grad_keys, grad_values, grad_weight)


def solution(mesh):
    in_specs = (
        P("seq", "fsdp"),
        P("seq", "fsdp"),
        P("seq", "fsdp"),
        P("seq"),
        P("fsdp", "seq"),
        P("seq", "fsdp"),
    )
    out_specs = (
        P("seq", "fsdp"),
        P("seq", "fsdp"),
        P("seq", "fsdp"),
        P("seq", "fsdp"),
        P("fsdp", "seq"),
    )
    return jax.shard_map(shards, mesh=mesh, in_specs=in_specs, out_specs=out_specs, check_vma=False)
```

profile of v0, /device:TPU:0, one launch (start us, length us, event | category | flops | bytes accessed | tf_op | source)
XLA Modules:
  0.0 683.8 jit_solution(8055189785752940412)
XLA Ops:
  11.6 10.4 %all-gather = s32[8,1,256]{2,1,0:T(1,128)S(1)} all-gather(s32[1,1,256]{2,1,0:T(1,128)S(1)} %bitcast.97), channel_id=1, replica_groups=mesh['seq'=8,'fsdp'=4] {'seq'}, dimensions={0}, use_global_device_ids=true | all-gather | bytes 9216 | tf_op jit(solution)/shard_map/all_gather | solution.py:65
  22.4 26.8 %all-gather.8.cloned.1.call-done = bf16[2048,1024]{1,0:T(8,128)(2,1)} async-done(((bf16[256,1024]{1,0:T(8,128)(2,1)}), bf16[2048,1024]{1,0:T(8,128)(2,1)}) %all-gather.8.cloned.1.call-update) | async-done | bytes 4194320 | tf_op jit(solution)/shard_map/all_gather | solution.py:64
  49.2 6.5 copy.42
  55.7 33.3 %all-gather.6.cloned.1.call-done = bf16[2048,1024]{0,1:T(8,128)(2,1)} async-done(((bf16[256,1024]{0,1:T(8,128)(2,1)}), bf16[2048,1024]{0,1:T(8,128)(2,1)}) %all-gather.6.cloned.1.call-update) | async-done | bytes 4194320 | tf_op jit(solution)/shard_map/all_gather | solution.py:63
  89.0 5.3 fusion.4
  94.3 4.5 exponential_reduce_fusion
  100.5 44.9 %all-gather.12.cloned.1.call-done = bf16[256,5120]{1,0:T(8,128)(2,1)} async-done(((bf16[256,1280]{1,0:T(8,128)(2,1)}), bf16[256,5120]{1,0:T(8,128)(2,1)}) %all-gather.12.cloned.1.call-update) | async-done | bytes 2621456 | tf_op jit(solution)/shard_map/all_gather | solution.py:80
  145.4 63.5 %all-gather.10.cloned.1.call-done = bf16[1024,5120]{1,0:T(8,128)(2,1)} async-done(((bf16[1024,640]{1,0:T(8,128)(2,1)}), bf16[1024,5120]{1,0:T(8,128)(2,1)}) %all-gather.10.cloned.1.call-update) | async-done | bytes 10485776 | tf_op jit(solution)/shard_map/all_gather | solution.py:73
  208.9 8.5 %convolution_convert_fusion.1 = bf16[256,1024]{1,0:T(8,128)(2,1)} fusion(bf16[256,5120]{1,0:T(8,128)(2,1)} %all-gather.12.cloned.1.call-done, bf16[1024,5120]{1,0:T(8,128)(2,1)} %all-gather.10.cloned.1.call-done), kind=kOutput, calls=%fused_computation.18 | convolution fusion | flops 2684616704 | bytes 13631488 | tf_op jit(solution)/shard_map/td,hd->th/dot_general | solution.py:81
  219.6 9.9 %multiply_reduce_fusion = (f32[256,8]{0,1:T(8,128)S(1)}, bf16[8,256,128]{1,2,0:T(8,128)(2,1)S(1)}) fusion(bf16[256,1024]{0,1:T(8,128)(2,1)} %copy.45, bf16[2048,8,128]{0,2,1:T(8,128)(2,1)} %bitcast.89, f32[8,256,2048]{2,1,0:T(8,128)} %copy-done, f32[8,256]{1,0:T(8,128)S(1)} %log_add_fusion, pred[256,2048]{1,0:T(8,128)(4,1)S(1)} %broadcast_compare_fusion.1), kind=kOutput, calls=%fused_computation.24 | convolution fusion | flops 1091827712 | bytes 22560768 | tf_op jit(solution)/shard_map/hqk,khd->qhd/dot_general | solution.py:68
  230.3 4.3 convolution_convert_fusion
  236.3 9.8 %fusion.10 = f32[1024,5120]{1,0:T(8,128)} fusion(bf16[256,1024]{0,1:T(8,128)(2,1)} %bitcast.91, bf16[256,5120]{1,0:T(8,128)(2,1)S(1)} %copy-done.3), kind=kOutput, calls=%fused_computation.30 | convolution fusion | flops 2684354560 | bytes 24117248 | tf_op jit(solution)/shard_map/th,td->hd/dot_general | solution.py:84
  251.9 416.6 %while.21 = (s32[]{:T(128)}, bf16[256,8,128]{2,0,1:T(8,128)(2,1)}, bf16[256,8,128]{2,0,1:T(8,128)(2,1)}, s32[256]{0:T(256)S(1)}, f32[256,8,128]{2,0,1:T(8,128)},...) while((s32[]{:T(128)}, bf16[256,8,128]{2,0,1:T(8,128)(2,1)}, ...), condition=%wide.region_5.6_spmd.clone, body=%wide.region_4.5_spmd.clone.sunk | while | flops 675872768 | bytes 34234708 | solution.py:110
  258.4 2.7 fusion.54
  265.4 30.6 %collective-permute-done.2 = s32[256]{0:T(256)S(1)} collective-permute-done((s32[256]{0:T(256)S(1)}, s32[256]{0:T(256)S(1)}, u32[]{:S(2)}, u32[]{:S(2)}) %collective-permute-start.2) | collective-permute-done | bytes 1056 | tf_op jit(solution)/shard_map/while/body/eval_jaxpr/ppermute | solution.py:13
  299.6 2.9 fusion.53
  302.4 2.9 fusion.54
  308.6 2.8 fusion.55
  311.4 43.0 %collective-permute-done.2 = s32[256]{0:T(256)S(1)} collective-permute-done((s32[256]{0:T(256)S(1)}, s32[256]{0:T(256)S(1)}, u32[]{:S(2)}, u32[]{:S(2)}) %collective-permute-start.2) | collective-permute-done | bytes 1056 | tf_op jit(solution)/shard_map/while/body/eval_jaxpr/ppermute | solution.py:13
  360.7 2.7 fusion.54
  365.1 3.4 collective-permute-start.1
  371.1 75.8 %collective-permute-done.2 = s32[256]{0:T(256)S(1)} collective-permute-done((s32[256]{0:T(256)S(1)}, s32[256]{0:T(256)S(1)}, u32[]{:S(2)}, u32[]{:S(2)}) %collective-permute-start.2) | collective-permute-done | bytes 1056 | tf_op jit(solution)/shard_map/while/body/eval_jaxpr/ppermute | solution.py:13
  457.5 3.4 collective-permute-start.1
  463.6 28.4 %collective-permute-done.2 = s32[256]{0:T(256)S(1)} collective-permute-done((s32[256]{0:T(256)S(1)}, s32[256]{0:T(256)S(1)}, u32[]{:S(2)}, u32[]{:S(2)}) %collective-permute-start.2) | collective-permute-done | bytes 1056 | tf_op jit(solution)/shard_map/while/body/eval_jaxpr/ppermute | solution.py:13
  501.6 3.5 collective-permute-start.1
  507.7 28.4 %collective-permute-done.2 = s32[256]{0:T(256)S(1)} collective-permute-done((s32[256]{0:T(256)S(1)}, s32[256]{0:T(256)S(1)}, u32[]{:S(2)}, u32[]{:S(2)}) %collective-permute-start.2) | collective-permute-done | bytes 1056 | tf_op jit(solution)/shard_map/while/body/eval_jaxpr/ppermute | solution.py:13
  545.7 3.4 collective-permute-start.1
  551.8 28.4 %collective-permute-done.2 = s32[256]{0:T(256)S(1)} collective-permute-done((s32[256]{0:T(256)S(1)}, s32[256]{0:T(256)S(1)}, u32[]{:S(2)}, u32[]{:S(2)}) %collective-permute-start.2) | collective-permute-done | bytes 1056 | tf_op jit(solution)/shard_map/while/body/eval_jaxpr/ppermute | solution.py:13
  589.8 3.4 collective-permute-start.1
  595.9 28.4 %collective-permute-done.2 = s32[256]{0:T(256)S(1)} collective-permute-done((s32[256]{0:T(256)S(1)}, s32[256]{0:T(256)S(1)}, u32[]{:S(2)}, u32[]{:S(2)}) %collective-permute-start.2) | collective-permute-done | bytes 1056 | tf_op jit(solution)/shard_map/while/body/eval_jaxpr/ppermute | solution.py:13
  633.9 3.4 collective-permute-start.1
  640.0 28.4 %collective-permute-done.2 = s32[256]{0:T(256)S(1)} collective-permute-done((s32[256]{0:T(256)S(1)}, s32[256]{0:T(256)S(1)}, u32[]{:S(2)}, u32[]{:S(2)}) %collective-permute-start.2) | collective-permute-done | bytes 1056 | tf_op jit(solution)/shard_map/while/body/eval_jaxpr/ppermute | solution.py:13
  (190 shorter events, 115.1 us)
Async XLA Ops:
  7.2 42.0 %all-gather.8.cloned.1.call-start = ((), (), s32[]{:S(2)}) async-start(), calls=%async_computation.3 | async-start | bytes 4718592 | tf_op jit(solution)/shard_map/all_gather | solution.py:64
  7.9 81.1 %all-gather.6.cloned.1.call-start = ((), (), s32[]{:S(2)}) async-start(), calls=%async_computation.2 | async-start | bytes 4718592 | tf_op jit(solution)/shard_map/all_gather | solution.py:63
  10.0 135.4 %all-gather.12.cloned.1.call-start = ((), (), s32[]{:S(2)}) async-start(), calls=%async_computation.6 | async-start | bytes 3276800 | tf_op jit(solution)/shard_map/all_gather | solution.py:80
  10.8 198.2 %all-gather.10.cloned.1.call-start = ((), (), s32[]{:S(2)}) async-start(), calls=%async_computation.4 | async-start | bytes 11796480 | tf_op jit(solution)/shard_map/all_gather | solution.py:73
  11.3 663.4 %reduce-scatter.3.cloned.1.call-start = ((), (), s32[]{:S(2)}) async-start(), calls=%async_computation.5 | async-start | bytes 3276800 | tf_op jit(solution)/shard_map/reduce_scatter | solution.py:77
  234.6 442.4 %reduce-scatter.5.cloned.1.call-start = ((), (), s32[]{:S(2)}) async-start(), calls=%async_computation.7 | async-start | bytes 23592960 | tf_op jit(solution)/shard_map/reduce_scatter | solution.py:87
  258.1 37.9 %collective-permute-start.3 = (f32[256,8,128]{2,0,1:T(8,128)}, f32[256,8,128]{2,0,1:T(8,128)}, u32[]{:S(2)}, u32[]{:S(2)}) collective-permute-start(f32[256,8,128]{2,0,1:T(8,128)} %fusion.53), channel_id=1, source_target_pairs={{28,0},{0,4},{4,8},{8,12},{12,16},{16,20},{20,24},{24,28},{29,1},{... | collective-permute-start | bytes 3145736 | tf_op jit(solution)/shard_map/while/body/eval_jaxpr/ppermute | solution.py:13
  302.4 52.0 %collective-permute-start.3 = (f32[256,8,128]{2,0,1:T(8,128)}, f32[256,8,128]{2,0,1:T(8,128)}, u32[]{:S(2)}, u32[]{:S(2)}) collective-permute-start(f32[256,8,128]{2,0,1:T(8,128)} %fusion.53), channel_id=1, source_target_pairs={{28,0},{0,4},{4,8},{8,12},{12,16},{16,20},{20,24},{24,28},{29,1},{... | collective-permute-start | bytes 3145736 | tf_op jit(solution)/shard_map/while/body/eval_jaxpr/ppermute | solution.py:13
  305.4 49.0 %collective-permute-start.4 = (f32[256,8,128]{2,0,1:T(8,128)}, f32[256,8,128]{2,0,1:T(8,128)}, u32[]{:S(2)}, u32[]{:S(2)}) collective-permute-start(f32[256,8,128]{2,0,1:T(8,128)} %fusion.54), channel_id=1, source_target_pairs={{28,0},{0,4},{4,8},{8,12},{12,16},{16,20},{20,24},{24,28},{29,1},{... | collective-permute-start | bytes 3145736 | tf_op jit(solution)/shard_map/while/body/eval_jaxpr/ppermute | solution.py:13
  306.3 48.0 %collective-permute-start = (bf16[256,8,128]{2,0,1:T(8,128)(2,1)S(1)}, bf16[256,8,128]{2,0,1:T(8,128)(2,1)}, u32[]{:S(2)}, u32[]{:S(2)}) collective-permute-start(bf16[256,8,128]{2,0,1:T(8,128)(2,1)S(1)} %copy.73), channel_id=1, source_target_pairs={{28,0},{0,4},{4,8},{8,12},{12,16},{16,20},{20,24},{24,28},{29,1},{... | collective-permute-start | bytes 1572872 | tf_op jit(solution)/shard_map/while/body/eval_jaxpr/ppermute | solution.py:13
  306.4 48.0 %collective-permute-start.1 = (bf16[256,8,128]{2,0,1:T(8,128)(2,1)S(1)}, bf16[256,8,128]{2,0,1:T(8,128)(2,1)}, u32[]{:S(2)}, u32[]{:S(2)}) collective-permute-start(bf16[256,8,128]{2,0,1:T(8,128)(2,1)S(1)} %copy.74), channel_id=1, source_target_pairs={{28,0},{0,4},{4,8},{8,12},{12,16},{16,20},{20,24},{24,28},{29,1},{... | collective-permute-start | bytes 1572872 | tf_op jit(solution)/shard_map/while/body/eval_jaxpr/ppermute | solution.py:13
  308.5 45.9 %collective-permute-start.2 = (s32[256]{0:T(256)S(1)}, s32[256]{0:T(256)S(1)}, u32[]{:S(2)}, u32[]{:S(2)}) collective-permute-start(s32[256]{0:T(256)S(1)} %copy.75), channel_id=1, source_target_pairs={{28,0},{0,4},{4,8},{8,12},{12,16},{16,20},{20,24},{24,28},{29,1},{... | collective-permute-start | bytes 3080 | tf_op jit(solution)/shard_map/while/body/eval_jaxpr/ppermute | solution.py:13
  360.7 86.3 %collective-permute-start.3 = (f32[256,8,128]{2,0,1:T(8,128)}, f32[256,8,128]{2,0,1:T(8,128)}, u32[]{:S(2)}, u32[]{:S(2)}) collective-permute-start(f32[256,8,128]{2,0,1:T(8,128)} %fusion.53), channel_id=1, source_target_pairs={{28,0},{0,4},{4,8},{8,12},{12,16},{16,20},{20,24},{24,28},{29,1},{... | collective-permute-start | bytes 3145736 | tf_op jit(solution)/shard_map/while/body/eval_jaxpr/ppermute | solution.py:13
  363.4 83.6 %collective-permute-start.4 = (f32[256,8,128]{2,0,1:T(8,128)}, f32[256,8,128]{2,0,1:T(8,128)}, u32[]{:S(2)}, u32[]{:S(2)}) collective-permute-start(f32[256,8,128]{2,0,1:T(8,128)} %fusion.54), channel_id=1, source_target_pairs={{28,0},{0,4},{4,8},{8,12},{12,16},{16,20},{20,24},{24,28},{29,1},{... | collective-permute-start | bytes 3145736 | tf_op jit(solution)/shard_map/while/body/eval_jaxpr/ppermute | solution.py:13
  364.7 82.3 %collective-permute-start = (bf16[256,8,128]{2,0,1:T(8,128)(2,1)S(1)}, bf16[256,8,128]{2,0,1:T(8,128)(2,1)}, u32[]{:S(2)}, u32[]{:S(2)}) collective-permute-start(bf16[256,8,128]{2,0,1:T(8,128)(2,1)S(1)} %copy.73), channel_id=1, source_target_pairs={{28,0},{0,4},{4,8},{8,12},{12,16},{16,20},{20,24},{24,28},{29,1},{... | collective-permute-start | bytes 1572872 | tf_op jit(solution)/shard_map/while/body/eval_jaxpr/ppermute | solution.py:13
  365.1 81.9 %collective-permute-start.1 = (bf16[256,8,128]{2,0,1:T(8,128)(2,1)S(1)}, bf16[256,8,128]{2,0,1:T(8,128)(2,1)}, u32[]{:S(2)}, u32[]{:S(2)}) collective-permute-start(bf16[256,8,128]{2,0,1:T(8,128)(2,1)S(1)} %copy.74), channel_id=1, source_target_pairs={{28,0},{0,4},{4,8},{8,12},{12,16},{16,20},{20,24},{24,28},{29,1},{... | collective-permute-start | bytes 1572872 | tf_op jit(solution)/shard_map/while/body/eval_jaxpr/ppermute | solution.py:13
  368.5 78.5 %collective-permute-start.2 = (s32[256]{0:T(256)S(1)}, s32[256]{0:T(256)S(1)}, u32[]{:S(2)}, u32[]{:S(2)}) collective-permute-start(s32[256]{0:T(256)S(1)} %copy.75), channel_id=1, source_target_pairs={{28,0},{0,4},{4,8},{8,12},{12,16},{16,20},{20,24},{24,28},{29,1},{... | collective-permute-start | bytes 3080 | tf_op jit(solution)/shard_map/while/body/eval_jaxpr/ppermute | solution.py:13
  453.2 38.9 %collective-permute-start.3 = (f32[256,8,128]{2,0,1:T(8,128)}, f32[256,8,128]{2,0,1:T(8,128)}, u32[]{:S(2)}, u32[]{:S(2)}) collective-permute-start(f32[256,8,128]{2,0,1:T(8,128)} %fusion.53), channel_id=1, source_target_pairs={{28,0},{0,4},{4,8},{8,12},{12,16},{16,20},{20,24},{24,28},{29,1},{... | collective-permute-start | bytes 3145736 | tf_op jit(solution)/shard_map/while/body/eval_jaxpr/ppermute | solution.py:13
  455.9 36.2 %collective-permute-start.4 = (f32[256,8,128]{2,0,1:T(8,128)}, f32[256,8,128]{2,0,1:T(8,128)}, u32[]{:S(2)}, u32[]{:S(2)}) collective-permute-start(f32[256,8,128]{2,0,1:T(8,128)} %fusion.54), channel_id=1, source_target_pairs={{28,0},{0,4},{4,8},{8,12},{12,16},{16,20},{20,24},{24,28},{29,1},{... | collective-permute-start | bytes 3145736 | tf_op jit(solution)/shard_map/while/body/eval_jaxpr/ppermute | solution.py:13
  457.0 35.0 %collective-permute-start = (bf16[256,8,128]{2,0,1:T(8,128)(2,1)S(1)}, bf16[256,8,128]{2,0,1:T(8,128)(2,1)}, u32[]{:S(2)}, u32[]{:S(2)}) collective-permute-start(bf16[256,8,128]{2,0,1:T(8,128)(2,1)S(1)} %copy.73), channel_id=1, source_target_pairs={{28,0},{0,4},{4,8},{8,12},{12,16},{16,20},{20,24},{24,28},{29,1},{... | collective-permute-start | bytes 1572872 | tf_op jit(solution)/shard_map/while/body/eval_jaxpr/ppermute | solution.py:13
  498.2 37.9 %collective-permute-start.3 = (f32[256,8,128]{2,0,1:T(8,128)}, f32[256,8,128]{2,0,1:T(8,128)}, u32[]{:S(2)}, u32[]{:S(2)}) collective-permute-start(f32[256,8,128]{2,0,1:T(8,128)} %fusion.53), channel_id=1, source_target_pairs={{28,0},{0,4},{4,8},{8,12},{12,16},{16,20},{20,24},{24,28},{29,1},{... | collective-permute-start | bytes 3145736 | tf_op jit(solution)/shard_map/while/body/eval_jaxpr/ppermute | solution.py:13
  501.0 35.2 %collective-permute-start.4 = (f32[256,8,128]{2,0,1:T(8,128)}, f32[256,8,128]{2,0,1:T(8,128)}, u32[]{:S(2)}, u32[]{:S(2)}) collective-permute-start(f32[256,8,128]{2,0,1:T(8,128)} %fusion.54), channel_id=1, source_target_pairs={{28,0},{0,4},{4,8},{8,12},{12,16},{16,20},{20,24},{24,28},{29,1},{... | collective-permute-start | bytes 3145736 | tf_op jit(solution)/shard_map/while/body/eval_jaxpr/ppermute | solution.py:13
  501.0 35.2 %collective-permute-start = (bf16[256,8,128]{2,0,1:T(8,128)(2,1)S(1)}, bf16[256,8,128]{2,0,1:T(8,128)(2,1)}, u32[]{:S(2)}, u32[]{:S(2)}) collective-permute-start(bf16[256,8,128]{2,0,1:T(8,128)(2,1)S(1)} %copy.73), channel_id=1, source_target_pairs={{28,0},{0,4},{4,8},{8,12},{12,16},{16,20},{20,24},{24,28},{29,1},{... | collective-permute-start | bytes 1572872 | tf_op jit(solution)/shard_map/while/body/eval_jaxpr/ppermute | solution.py:13
  542.3 37.9 %collective-permute-start.3 = (f32[256,8,128]{2,0,1:T(8,128)}, f32[256,8,128]{2,0,1:T(8,128)}, u32[]{:S(2)}, u32[]{:S(2)}) collective-permute-start(f32[256,8,128]{2,0,1:T(8,128)} %fusion.53), channel_id=1, source_target_pairs={{28,0},{0,4},{4,8},{8,12},{12,16},{16,20},{20,24},{24,28},{29,1},{... | collective-permute-start | bytes 3145736 | tf_op jit(solution)/shard_map/while/body/eval_jaxpr/ppermute | solution.py:13
  545.1 35.2 %collective-permute-start.4 = (f32[256,8,128]{2,0,1:T(8,128)}, f32[256,8,128]{2,0,1:T(8,128)}, u32[]{:S(2)}, u32[]{:S(2)}) collective-permute-start(f32[256,8,128]{2,0,1:T(8,128)} %fusion.54), channel_id=1, source_target_pairs={{28,0},{0,4},{4,8},{8,12},{12,16},{16,20},{20,24},{24,28},{29,1},{... | collective-permute-start | bytes 3145736 | tf_op jit(solution)/shard_map/while/body/eval_jaxpr/ppermute | solution.py:13
  545.1 35.2 %collective-permute-start = (bf16[256,8,128]{2,0,1:T(8,128)(2,1)S(1)}, bf16[256,8,128]{2,0,1:T(8,128)(2,1)}, u32[]{:S(2)}, u32[]{:S(2)}) collective-permute-start(bf16[256,8,128]{2,0,1:T(8,128)(2,1)S(1)} %copy.73), channel_id=1, source_target_pairs={{28,0},{0,4},{4,8},{8,12},{12,16},{16,20},{20,24},{24,28},{29,1},{... | collective-permute-start | bytes 1572872 | tf_op jit(solution)/shard_map/while/body/eval_jaxpr/ppermute | solution.py:13
  586.4 37.9 %collective-permute-start.3 = (f32[256,8,128]{2,0,1:T(8,128)}, f32[256,8,128]{2,0,1:T(8,128)}, u32[]{:S(2)}, u32[]{:S(2)}) collective-permute-start(f32[256,8,128]{2,0,1:T(8,128)} %fusion.53), channel_id=1, source_target_pairs={{28,0},{0,4},{4,8},{8,12},{12,16},{16,20},{20,24},{24,28},{29,1},{... | collective-permute-start | bytes 3145736 | tf_op jit(solution)/shard_map/while/body/eval_jaxpr/ppermute | solution.py:13
  589.2 35.2 %collective-permute-start.4 = (f32[256,8,128]{2,0,1:T(8,128)}, f32[256,8,128]{2,0,1:T(8,128)}, u32[]{:S(2)}, u32[]{:S(2)}) collective-permute-start(f32[256,8,128]{2,0,1:T(8,128)} %fusion.54), channel_id=1, source_target_pairs={{28,0},{0,4},{4,8},{8,12},{12,16},{16,20},{20,24},{24,28},{29,1},{... | collective-permute-start | bytes 3145736 | tf_op jit(solution)/shard_map/while/body/eval_jaxpr/ppermute | solution.py:13
  589.2 35.2 %collective-permute-start = (bf16[256,8,128]{2,0,1:T(8,128)(2,1)S(1)}, bf16[256,8,128]{2,0,1:T(8,128)(2,1)}, u32[]{:S(2)}, u32[]{:S(2)}) collective-permute-start(bf16[256,8,128]{2,0,1:T(8,128)(2,1)S(1)} %copy.73), channel_id=1, source_target_pairs={{28,0},{0,4},{4,8},{8,12},{12,16},{16,20},{20,24},{24,28},{29,1},{... | collective-permute-start | bytes 1572872 | tf_op jit(solution)/shard_map/while/body/eval_jaxpr/ppermute | solution.py:13
  630.5 37.9 %collective-permute-start.3 = (f32[256,8,128]{2,0,1:T(8,128)}, f32[256,8,128]{2,0,1:T(8,128)}, u32[]{:S(2)}, u32[]{:S(2)}) collective-permute-start(f32[256,8,128]{2,0,1:T(8,128)} %fusion.53), channel_id=1, source_target_pairs={{28,0},{0,4},{4,8},{8,12},{12,16},{16,20},{20,24},{24,28},{29,1},{... | collective-permute-start | bytes 3145736 | tf_op jit(solution)/shard_map/while/body/eval_jaxpr/ppermute | solution.py:13
  633.3 35.2 %collective-permute-start.4 = (f32[256,8,128]{2,0,1:T(8,128)}, f32[256,8,128]{2,0,1:T(8,128)}, u32[]{:S(2)}, u32[]{:S(2)}) collective-permute-start(f32[256,8,128]{2,0,1:T(8,128)} %fusion.54), channel_id=1, source_target_pairs={{28,0},{0,4},{4,8},{8,12},{12,16},{16,20},{20,24},{24,28},{29,1},{... | collective-permute-start | bytes 3145736 | tf_op jit(solution)/shard_map/while/body/eval_jaxpr/ppermute | solution.py:13
  633.3 35.2 %collective-permute-start = (bf16[256,8,128]{2,0,1:T(8,128)(2,1)S(1)}, bf16[256,8,128]{2,0,1:T(8,128)(2,1)}, u32[]{:S(2)}, u32[]{:S(2)}) collective-permute-start(bf16[256,8,128]{2,0,1:T(8,128)(2,1)S(1)} %copy.73), channel_id=1, source_target_pairs={{28,0},{0,4},{4,8},{8,12},{12,16},{16,20},{20,24},{24,28},{29,1},{... | collective-permute-start | bytes 1572872 | tf_op jit(solution)/shard_map/while/body/eval_jaxpr/ppermute | solution.py:13
  (25 other events, 519.3 us)
Sparse Core Ops, SparseCore 0:
  9.9 39.2 all-gather.7
  51.7 37.3 all-gather.5
  90.6 54.7 all-gather.11
  147.2 61.7 all-gather.9
  234.7 52.2 reduce-scatter.2
  291.1 169.2 reduce-scatter.4
where the time goes:
time: 686 us; the launch traced here: 684 us
  waiting for transfers between devices  462 us (67%)
  matrix products  111 us (16%)
  local copies, waits for them, and re-layouts  41.9 us (6%)
  starting transfers between devices  33.5 us (5%)
  between operations  14.3 us (2%)
  blocking collectives  10.4 us (2%)
  other arithmetic  9.66 us (1%)
    ppermute x40, waiting for transfers between devices, shifted(): return lax.ppermute(block, axis, route)  292 us
    all_gather x1, waiting for transfers between devices, shards(): weight_full = lax.all_gather(out_weight, 'seq', axis=1, tiled=True)  63.5 us
    all_gather x1, waiting for transfers between devices, shards(): cotangent_full = lax.all_gather(cotangent, 'fsdp', axis=1, tiled=True)  44.9 us
    all_gather x1, waiting for transfers between devices, shards(): piece_keys = lax.all_gather(key_states, 'seq', axis=0, tiled=True)  33.3 us
    ppermute x40, starting transfers between devices, shifted(): return lax.ppermute(block, axis, route)  33.1 us
    all_gather x1, waiting for transfers between devices, shards(): piece_values = lax.all_gather(value_states, 'seq', axis=0, tiled=True)  26.8 us
    dot_general x8, matrix products, tile_grads(): jnp.einsum('hqk,qhd->khd', probs.astype(jnp.bfloat16), grad_rows, preferr...  22 us
    dot_general x8, matrix products, tile_grads(): jnp.einsum('hqk,qhd->khd', grad_scores, query_rows, preferred_element_typ...  21.7 us
  transfers between devices with their start and end apart: 46, of which 12 were waited for; matrix products, arithmetic and copies ran while one was open for 20% of the time, Pallas kernels for 0%

commit v1 on v0

--- a/solution.py
+++ b/solution.py
@@ -77,7 +77,23 @@
     attn_output = lax.psum_scatter(partial_sum, "fsdp", scatter_dimension=1, tiled=True).astype(
         jnp.float32
     )
-    cotangent_full = lax.all_gather(cotangent, "fsdp", axis=1, tiled=True)
+    ways, here, step = (lax.axis_size("fsdp"), lax.axis_index("fsdp"), cotangent.shape[1])
+    shape = [n * ways if d == 1 else n for d, n in enumerate(cotangent.shape)]
+    full = lax.dynamic_update_slice_in_dim(
+        jnp.zeros(shape, cotangent.dtype), cotangent, here * step, axis=1
+    )
+    going_up = going_down = cotangent
+    for far in range(1, ways // 2 + 1):
+        going_up = lax.ppermute(going_up, "fsdp", [(d, (d + 1) % ways) for d in range(ways)])
+        full = lax.dynamic_update_slice_in_dim(full, going_up, (here - far) % ways * step, axis=1)
+        if 2 * far < ways:
+            going_down = lax.ppermute(
+                going_down, "fsdp", [(d, (d - 1) % ways) for d in range(ways)]
+            )
+            full = lax.dynamic_update_slice_in_dim(
+                full, going_down, (here + far) % ways * step, axis=1
+            )
+    cotangent_full = full
     grad_attended = jnp.einsum(
         "td,hd->th", cotangent_full, weight_full, preferred_element_type=jnp.float32
     ).astype(jnp.bfloat16)

time: 686 us -> 630 us (0.918)
  waiting for transfers between devices: 462 us -> 395 us
    all_gather x1 -> x0, waiting for transfers between devices: 44.9 us -> none  [shards(): cotangent_full = lax.all_gather(cotangent, 'fsdp', axis=1, tiled=True)]
    ppermute x0 -> x3, waiting for transfers between devices: none -> 27.7 us  [the longest x2 17.7 us: shards(): lax.ppermute(going_up, 'fsdp', [(d, (d + 1) % ways) for d in range(ways)])]
    all_gather x1, waiting for transfers between devices: 26.8 us -> 0.02 us  [shards(): piece_values = lax.all_gather(value_states, 'seq', axis=0, tiled=True)]
    all_gather x1, waiting for transfers between devices: 63.5 us -> 52.6 us  [shards(): weight_full = lax.all_gather(out_weight, 'seq', axis=1, tiled=True)]
    all_gather x1, waiting for transfers between devices: 33.3 us -> 23 us  [shards(): piece_keys = lax.all_gather(key_states, 'seq', axis=0, tiled=True)]
  transfers between devices with their start and end apart: 46 -> 48, of which waited for: 12 -> 13; matrix products, arithmetic and copies ran while one was open for 20% -> 22% of each run, Pallas kernels for 0% -> 0%
where the time goes in v1:
time: 630 us; the launch traced here: 628 us
  waiting for transfers between devices  395 us (63%)
  matrix products  111 us (18%)
  local copies, waits for them, and re-layouts  48.1 us (8%)
  starting transfers between devices  40.1 us (6%)
  between operations  14.1 us (2%)
  other arithmetic  10.3 us (2%)
  blocking collectives  9.26 us (1%)
    ppermute x40, waiting for transfers between devices, shifted(): return lax.ppermute(block, axis, route)  290 us
    all_gather x1, waiting for transfers between devices, shards(): weight_full = lax.all_gather(out_weight, 'seq', axis=1, tiled=True)  52.6 us
    ppermute x40, starting transfers between devices, shifted(): return lax.ppermute(block, axis, route)  34.5 us
    all_gather x1, waiting for transfers between devices, shards(): piece_keys = lax.all_gather(key_states, 'seq', axis=0, tiled=True)  23 us
    dot_general x8, matrix products, tile_grads(): jnp.einsum('hqk,qhd->khd', grad_scores, query_rows, preferred_element_typ...  21.9 us
    dot_general x8, matrix products, tile_grads(): jnp.einsum('hqk,qhd->khd', probs.astype(jnp.bfloat16), grad_rows, preferr...  21.9 us
    dot_general x8, matrix products, tile_grads(): jnp.einsum('hqk,khd->qhd', grad_scores, key_rows, preferred_element_type=...  19.9 us
    ppermute x2, waiting for transfers between devices, shards(): lax.ppermute(going_up, 'fsdp', [(d, (d + 1) % ways) for d in range(ways)])  17.7 us
  transfers between devices with their start and end apart: 48, of which 13 were waited for; matrix products, arithmetic and copies ran while one was open for 22% of the time, Pallas kernels for 0%

profile of v1, /device:TPU:0, one launch (start us, length us, event | category | flops | bytes accessed | tf_op | source)
XLA Modules:
  0.0 628.0 jit_solution(5550214032742958116)
XLA Ops:
  10.8 3.1 collective-permute-start.5
  16.0 9.3 %all-gather = s32[8,1,256]{2,1,0:T(1,128)S(1)} all-gather(s32[1,1,256]{2,1,0:T(1,128)} %bitcast.97), channel_id=1, replica_groups=mesh['seq'=8,'fsdp'=4] {'seq'}, dimensions={0}, use_global_device_ids=true | all-gather | bytes 9216 | tf_op jit(solution)/shard_map/all_gather | solution.py:65
  27.4 4.5 collective-permute-done.5
  34.7 10.0 %collective-permute-done.6 = bf16[256,1280]{1,0:T(8,128)(2,1)} collective-permute-done((bf16[256,1280]{1,0:T(8,128)(2,1)}, bf16[256,1280]{1,0:T(8,128)(2,1)}, u32[]{:S(2)}, u32[]{:S(2)}) %collective-permute-start.6) | collective-permute-done | bytes 655392 | tf_op jit(solution)/shard_map/ppermute | solution.py:90
  45.9 13.1 %collective-permute-done.7 = bf16[256,1280]{1,0:T(8,128)(2,1)S(1)} collective-permute-done((bf16[256,1280]{1,0:T(8,128)(2,1)}, bf16[256,1280]{1,0:T(8,128)(2,1)S(1)}, u32[]{:S(2)}, u32[]{:S(2)}) %collective-permute-start.7) | collective-permute-done | bytes 655392 | tf_op jit(solution)/shard_map/ppermute | solution.py:87
  59.1 6.9 %copy.42 = bf16[2048,1024]{0,1:T(8,128)(2,1)} copy(bf16[2048,1024]{1,0:T(8,128)(2,1)} %all-gather.7.cloned.1.call-done) | data formatting | bytes 8388608 | tf_op jit(solution)/shard_map/all_gather | solution.py:64
  66.1 23.0 %all-gather.5.cloned.1.call-done = bf16[2048,1024]{0,1:T(8,128)(2,1)} async-done(((bf16[256,1024]{0,1:T(8,128)(2,1)}), bf16[2048,1024]{0,1:T(8,128)(2,1)}) %all-gather.5.cloned.1.call-update) | async-done | bytes 4194320 | tf_op jit(solution)/shard_map/all_gather | solution.py:63
  89.0 5.4 fusion.4
  94.5 4.5 exponential_reduce_fusion
  101.4 52.6 %all-gather.9.cloned.1.call-done = bf16[1024,5120]{1,0:T(8,128)(2,1)} async-done(((bf16[1024,640]{1,0:T(8,128)(2,1)}), bf16[1024,5120]{1,0:T(8,128)(2,1)}) %all-gather.9.cloned.1.call-update) | async-done | bytes 10485776 | tf_op jit(solution)/shard_map/all_gather | solution.py:73
  154.0 7.7 %convolution_convert_fusion.1 = bf16[256,1024]{1,0:T(8,128)(2,1)} fusion(bf16[256,5120]{1,0:T(8,128)(2,1)S(1)} %constant_dynamic-update-slice_fusion, bf16[1024,5120]{1,0:T(8,128)(2,1)} %all-gather.9.cloned.1.call-done), kind=kOutput, calls=%fused_computation.18 | convolution fusion | flops 2684616704 | bytes 13631488 | tf_op jit(solution)/shard_map/td,hd->th/dot_general | solution.py:97
  163.8 9.9 %multiply_reduce_fusion = (f32[256,8]{0,1:T(8,128)S(1)}, bf16[8,256,128]{1,2,0:T(8,128)(2,1)S(1)}) fusion(bf16[256,1024]{0,1:T(8,128)(2,1)} %copy.45, bf16[2048,8,128]{0,2,1:T(8,128)(2,1)} %bitcast.89, f32[8,256,2048]{2,1,0:T(8,128)} %copy-done, f32[8,256]{1,0:T(8,128)S(1)} %log_add_fusion, pred[256,2048]{1,0:T(8,128)(4,1)S(1)} %broadcast_compare_fusion.1), kind=kOutput, calls=%fused_computation.24 | convolution fusion | flops 1091827712 | bytes 22560768 | tf_op jit(solution)/shard_map/hqk,khd->qhd/dot_general | solution.py:68
  174.6 4.3 convolution_convert_fusion
  180.6 9.8 %fusion.10 = f32[1024,5120]{1,0:T(8,128)} fusion(bf16[256,1024]{0,1:T(8,128)(2,1)} %bitcast.91, bf16[256,5120]{1,0:T(8,128)(2,1)S(1)} %copy-done.2), kind=kOutput, calls=%fused_computation.34 | convolution fusion | flops 2684354560 | bytes 24117248 | tf_op jit(solution)/shard_map/th,td->hd/dot_general | solution.py:100
  196.4 416.6 %while.21 = (s32[]{:T(128)}, bf16[256,8,128]{2,0,1:T(8,128)(2,1)}, bf16[256,8,128]{2,0,1:T(8,128)(2,1)}, s32[256]{0:T(256)S(1)}, f32[256,8,128]{2,0,1:T(8,128)},...) while((s32[]{:T(128)}, bf16[256,8,128]{2,0,1:T(8,128)(2,1)}, ...), condition=%wide.region_5.6_spmd.clone, body=%wide.region_4.5_spmd.clone.sunk | while | flops 675872768 | bytes 34234708 | solution.py:126
  209.8 30.6 %collective-permute-done.2 = s32[256]{0:T(256)S(1)} collective-permute-done((s32[256]{0:T(256)S(1)}, s32[256]{0:T(256)S(1)}, u32[]{:S(2)}, u32[]{:S(2)}) %collective-permute-start.2) | collective-permute-done | bytes 1056 | tf_op jit(solution)/shard_map/while/body/eval_jaxpr/ppermute | solution.py:13
  244.0 3.0 fusion.53
  246.9 2.9 fusion.54
  255.9 43.7 %collective-permute-done.2 = s32[256]{0:T(256)S(1)} collective-permute-done((s32[256]{0:T(256)S(1)}, s32[256]{0:T(256)S(1)}, u32[]{:S(2)}, u32[]{:S(2)}) %collective-permute-start.2) | collective-permute-done | bytes 1056 | tf_op jit(solution)/shard_map/while/body/eval_jaxpr/ppermute | solution.py:13
  303.1 2.8 fusion.53
  310.0 3.5 collective-permute-start.1
  316.1 75.9 %collective-permute-done.2 = s32[256]{0:T(256)S(1)} collective-permute-done((s32[256]{0:T(256)S(1)}, s32[256]{0:T(256)S(1)}, u32[]{:S(2)}, u32[]{:S(2)}) %collective-permute-start.2) | collective-permute-done | bytes 1056 | tf_op jit(solution)/shard_map/while/body/eval_jaxpr/ppermute | solution.py:13
  402.5 3.4 collective-permute-start.1
  408.6 28.0 %collective-permute-done.2 = s32[256]{0:T(256)S(1)} collective-permute-done((s32[256]{0:T(256)S(1)}, s32[256]{0:T(256)S(1)}, u32[]{:S(2)}, u32[]{:S(2)}) %collective-permute-start.2) | collective-permute-done | bytes 1056 | tf_op jit(solution)/shard_map/while/body/eval_jaxpr/ppermute | solution.py:13
  446.6 3.4 collective-permute-start.1
  452.7 28.0 %collective-permute-done.2 = s32[256]{0:T(256)S(1)} collective-permute-done((s32[256]{0:T(256)S(1)}, s32[256]{0:T(256)S(1)}, u32[]{:S(2)}, u32[]{:S(2)}) %collective-permute-start.2) | collective-permute-done | bytes 1056 | tf_op jit(solution)/shard_map/while/body/eval_jaxpr/ppermute | solution.py:13
  490.7 3.4 collective-permute-start.1
  496.8 28.0 %collective-permute-done.2 = s32[256]{0:T(256)S(1)} collective-permute-done((s32[256]{0:T(256)S(1)}, s32[256]{0:T(256)S(1)}, u32[]{:S(2)}, u32[]{:S(2)}) %collective-permute-start.2) | collective-permute-done | bytes 1056 | tf_op jit(solution)/shard_map/while/body/eval_jaxpr/ppermute | solution.py:13
  534.8 3.4 collective-permute-start.1
  540.9 28.0 %collective-permute-done.2 = s32[256]{0:T(256)S(1)} collective-permute-done((s32[256]{0:T(256)S(1)}, s32[256]{0:T(256)S(1)}, u32[]{:S(2)}, u32[]{:S(2)}) %collective-permute-start.2) | collective-permute-done | bytes 1056 | tf_op jit(solution)/shard_map/while/body/eval_jaxpr/ppermute | solution.py:13
  578.9 3.4 collective-permute-start.1
  585.0 28.0 %collective-permute-done.2 = s32[256]{0:T(256)S(1)} collective-permute-done((s32[256]{0:T(256)S(1)}, s32[256]{0:T(256)S(1)}, u32[]{:S(2)}, u32[]{:S(2)}) %collective-permute-start.2) | collective-permute-done | bytes 1056 | tf_op jit(solution)/shard_map/while/body/eval_jaxpr/ppermute | solution.py:13
  (202 shorter events, 129.9 us)
Async XLA Ops:
  7.2 52.0 %all-gather.7.cloned.1.call-start = ((), (), s32[]{:S(2)}) async-start(), calls=%async_computation.3 | async-start | bytes 4718592 | tf_op jit(solution)/shard_map/all_gather | solution.py:64
  7.9 81.1 %all-gather.5.cloned.1.call-start = ((), (), s32[]{:S(2)}) async-start(), calls=%async_computation.2 | async-start | bytes 4718592 | tf_op jit(solution)/shard_map/all_gather | solution.py:63
  10.0 143.9 %all-gather.9.cloned.1.call-start = ((), (), s32[]{:S(2)}) async-start(), calls=%async_computation.4 | async-start | bytes 11796480 | tf_op jit(solution)/shard_map/all_gather | solution.py:73
  10.8 608.5 %reduce-scatter.3.cloned.1.call-start = ((), (), s32[]{:S(2)}) async-start(), calls=%async_computation.5 | async-start | bytes 3276800 | tf_op jit(solution)/shard_map/reduce_scatter | solution.py:77
  178.8 442.6 %reduce-scatter.5.cloned.1.call-start = ((), (), s32[]{:S(2)}) async-start(), calls=%async_computation.6 | async-start | bytes 23592960 | tf_op jit(solution)/shard_map/reduce_scatter | solution.py:103
  202.5 37.9 %collective-permute-start.3 = (f32[256,8,128]{2,0,1:T(8,128)}, f32[256,8,128]{2,0,1:T(8,128)}, u32[]{:S(2)}, u32[]{:S(2)}) collective-permute-start(f32[256,8,128]{2,0,1:T(8,128)} %fusion.53), channel_id=1, source_target_pairs={{28,0},{0,4},{4,8},{8,12},{12,16},{16,20},{20,24},{24,28},{29,1},{... | collective-permute-start | bytes 3145736 | tf_op jit(solution)/shard_map/while/body/eval_jaxpr/ppermute | solution.py:13
  205.6 34.9 %collective-permute-start.4 = (f32[256,8,128]{2,0,1:T(8,128)}, f32[256,8,128]{2,0,1:T(8,128)}, u32[]{:S(2)}, u32[]{:S(2)}) collective-permute-start(f32[256,8,128]{2,0,1:T(8,128)} %fusion.54), channel_id=1, source_target_pairs={{28,0},{0,4},{4,8},{8,12},{12,16},{16,20},{20,24},{24,28},{29,1},{... | collective-permute-start | bytes 3145736 | tf_op jit(solution)/shard_map/while/body/eval_jaxpr/ppermute | solution.py:13
  246.9 52.6 %collective-permute-start.3 = (f32[256,8,128]{2,0,1:T(8,128)}, f32[256,8,128]{2,0,1:T(8,128)}, u32[]{:S(2)}, u32[]{:S(2)}) collective-permute-start(f32[256,8,128]{2,0,1:T(8,128)} %fusion.53), channel_id=1, source_target_pairs={{28,0},{0,4},{4,8},{8,12},{12,16},{16,20},{20,24},{24,28},{29,1},{... | collective-permute-start | bytes 3145736 | tf_op jit(solution)/shard_map/while/body/eval_jaxpr/ppermute | solution.py:13
  249.8 49.8 %collective-permute-start.4 = (f32[256,8,128]{2,0,1:T(8,128)}, f32[256,8,128]{2,0,1:T(8,128)}, u32[]{:S(2)}, u32[]{:S(2)}) collective-permute-start(f32[256,8,128]{2,0,1:T(8,128)} %fusion.54), channel_id=1, source_target_pairs={{28,0},{0,4},{4,8},{8,12},{12,16},{16,20},{20,24},{24,28},{29,1},{... | collective-permute-start | bytes 3145736 | tf_op jit(solution)/shard_map/while/body/eval_jaxpr/ppermute | solution.py:13
  250.8 48.7 %collective-permute-start = (bf16[256,8,128]{2,0,1:T(8,128)(2,1)S(1)}, bf16[256,8,128]{2,0,1:T(8,128)(2,1)}, u32[]{:S(2)}, u32[]{:S(2)}) collective-permute-start(bf16[256,8,128]{2,0,1:T(8,128)(2,1)S(1)} %copy.77), channel_id=1, source_target_pairs={{28,0},{0,4},{4,8},{8,12},{12,16},{16,20},{20,24},{24,28},{29,1},{... | collective-permute-start | bytes 1572872 | tf_op jit(solution)/shard_map/while/body/eval_jaxpr/ppermute | solution.py:13
  250.8 48.7 %collective-permute-start.1 = (bf16[256,8,128]{2,0,1:T(8,128)(2,1)S(1)}, bf16[256,8,128]{2,0,1:T(8,128)(2,1)}, u32[]{:S(2)}, u32[]{:S(2)}) collective-permute-start(bf16[256,8,128]{2,0,1:T(8,128)(2,1)S(1)} %copy.78), channel_id=1, source_target_pairs={{28,0},{0,4},{4,8},{8,12},{12,16},{16,20},{20,24},{24,28},{29,1},{... | collective-permute-start | bytes 1572872 | tf_op jit(solution)/shard_map/while/body/eval_jaxpr/ppermute | solution.py:13
  253.1 46.5 %collective-permute-start.2 = (s32[256]{0:T(256)S(1)}, s32[256]{0:T(256)S(1)}, u32[]{:S(2)}, u32[]{:S(2)}) collective-permute-start(s32[256]{0:T(256)S(1)} %copy.79), channel_id=1, source_target_pairs={{28,0},{0,4},{4,8},{8,12},{12,16},{16,20},{20,24},{24,28},{29,1},{... | collective-permute-start | bytes 3080 | tf_op jit(solution)/shard_map/while/body/eval_jaxpr/ppermute | solution.py:13
  306.0 86.1 %collective-permute-start.3 = (f32[256,8,128]{2,0,1:T(8,128)}, f32[256,8,128]{2,0,1:T(8,128)}, u32[]{:S(2)}, u32[]{:S(2)}) collective-permute-start(f32[256,8,128]{2,0,1:T(8,128)} %fusion.53), channel_id=1, source_target_pairs={{28,0},{0,4},{4,8},{8,12},{12,16},{16,20},{20,24},{24,28},{29,1},{... | collective-permute-start | bytes 3145736 | tf_op jit(solution)/shard_map/while/body/eval_jaxpr/ppermute | solution.py:13
  308.7 83.4 %collective-permute-start.4 = (f32[256,8,128]{2,0,1:T(8,128)}, f32[256,8,128]{2,0,1:T(8,128)}, u32[]{:S(2)}, u32[]{:S(2)}) collective-permute-start(f32[256,8,128]{2,0,1:T(8,128)} %fusion.54), channel_id=1, source_target_pairs={{28,0},{0,4},{4,8},{8,12},{12,16},{16,20},{20,24},{24,28},{29,1},{... | collective-permute-start | bytes 3145736 | tf_op jit(solution)/shard_map/while/body/eval_jaxpr/ppermute | solution.py:13
  309.9 82.2 %collective-permute-start = (bf16[256,8,128]{2,0,1:T(8,128)(2,1)S(1)}, bf16[256,8,128]{2,0,1:T(8,128)(2,1)}, u32[]{:S(2)}, u32[]{:S(2)}) collective-permute-start(bf16[256,8,128]{2,0,1:T(8,128)(2,1)S(1)} %copy.77), channel_id=1, source_target_pairs={{28,0},{0,4},{4,8},{8,12},{12,16},{16,20},{20,24},{24,28},{29,1},{... | collective-permute-start | bytes 1572872 | tf_op jit(solution)/shard_map/while/body/eval_jaxpr/ppermute | solution.py:13
  310.0 82.0 %collective-permute-start.1 = (bf16[256,8,128]{2,0,1:T(8,128)(2,1)S(1)}, bf16[256,8,128]{2,0,1:T(8,128)(2,1)}, u32[]{:S(2)}, u32[]{:S(2)}) collective-permute-start(bf16[256,8,128]{2,0,1:T(8,128)(2,1)S(1)} %copy.78), channel_id=1, source_target_pairs={{28,0},{0,4},{4,8},{8,12},{12,16},{16,20},{20,24},{24,28},{29,1},{... | collective-permute-start | bytes 1572872 | tf_op jit(solution)/shard_map/while/body/eval_jaxpr/ppermute | solution.py:13
  313.5 78.6 %collective-permute-start.2 = (s32[256]{0:T(256)S(1)}, s32[256]{0:T(256)S(1)}, u32[]{:S(2)}, u32[]{:S(2)}) collective-permute-start(s32[256]{0:T(256)S(1)} %copy.79), channel_id=1, source_target_pairs={{28,0},{0,4},{4,8},{8,12},{12,16},{16,20},{20,24},{24,28},{29,1},{... | collective-permute-start | bytes 3080 | tf_op jit(solution)/shard_map/while/body/eval_jaxpr/ppermute | solution.py:13
  398.3 38.3 %collective-permute-start.3 = (f32[256,8,128]{2,0,1:T(8,128)}, f32[256,8,128]{2,0,1:T(8,128)}, u32[]{:S(2)}, u32[]{:S(2)}) collective-permute-start(f32[256,8,128]{2,0,1:T(8,128)} %fusion.53), channel_id=1, source_target_pairs={{28,0},{0,4},{4,8},{8,12},{12,16},{16,20},{20,24},{24,28},{29,1},{... | collective-permute-start | bytes 3145736 | tf_op jit(solution)/shard_map/while/body/eval_jaxpr/ppermute | solution.py:13
  401.0 35.5 %collective-permute-start.4 = (f32[256,8,128]{2,0,1:T(8,128)}, f32[256,8,128]{2,0,1:T(8,128)}, u32[]{:S(2)}, u32[]{:S(2)}) collective-permute-start(f32[256,8,128]{2,0,1:T(8,128)} %fusion.54), channel_id=1, source_target_pairs={{28,0},{0,4},{4,8},{8,12},{12,16},{16,20},{20,24},{24,28},{29,1},{... | collective-permute-start | bytes 3145736 | tf_op jit(solution)/shard_map/while/body/eval_jaxpr/ppermute | solution.py:13
  402.3 34.2 %collective-permute-start = (bf16[256,8,128]{2,0,1:T(8,128)(2,1)S(1)}, bf16[256,8,128]{2,0,1:T(8,128)(2,1)}, u32[]{:S(2)}, u32[]{:S(2)}) collective-permute-start(bf16[256,8,128]{2,0,1:T(8,128)(2,1)S(1)} %copy.77), channel_id=1, source_target_pairs={{28,0},{0,4},{4,8},{8,12},{12,16},{16,20},{20,24},{24,28},{29,1},{... | collective-permute-start | bytes 1572872 | tf_op jit(solution)/shard_map/while/body/eval_jaxpr/ppermute | solution.py:13
  442.8 37.9 %collective-permute-start.3 = (f32[256,8,128]{2,0,1:T(8,128)}, f32[256,8,128]{2,0,1:T(8,128)}, u32[]{:S(2)}, u32[]{:S(2)}) collective-permute-start(f32[256,8,128]{2,0,1:T(8,128)} %fusion.53), channel_id=1, source_target_pairs={{28,0},{0,4},{4,8},{8,12},{12,16},{16,20},{20,24},{24,28},{29,1},{... | collective-permute-start | bytes 3145736 | tf_op jit(solution)/shard_map/while/body/eval_jaxpr/ppermute | solution.py:13
  445.5 35.2 %collective-permute-start.4 = (f32[256,8,128]{2,0,1:T(8,128)}, f32[256,8,128]{2,0,1:T(8,128)}, u32[]{:S(2)}, u32[]{:S(2)}) collective-permute-start(f32[256,8,128]{2,0,1:T(8,128)} %fusion.54), channel_id=1, source_target_pairs={{28,0},{0,4},{4,8},{8,12},{12,16},{16,20},{20,24},{24,28},{29,1},{... | collective-permute-start | bytes 3145736 | tf_op jit(solution)/shard_map/while/body/eval_jaxpr/ppermute | solution.py:13
  445.6 35.1 %collective-permute-start = (bf16[256,8,128]{2,0,1:T(8,128)(2,1)S(1)}, bf16[256,8,128]{2,0,1:T(8,128)(2,1)}, u32[]{:S(2)}, u32[]{:S(2)}) collective-permute-start(bf16[256,8,128]{2,0,1:T(8,128)(2,1)S(1)} %copy.77), channel_id=1, source_target_pairs={{28,0},{0,4},{4,8},{8,12},{12,16},{16,20},{20,24},{24,28},{29,1},{... | collective-permute-start | bytes 1572872 | tf_op jit(solution)/shard_map/while/body/eval_jaxpr/ppermute | solution.py:13
  486.9 37.9 %collective-permute-start.3 = (f32[256,8,128]{2,0,1:T(8,128)}, f32[256,8,128]{2,0,1:T(8,128)}, u32[]{:S(2)}, u32[]{:S(2)}) collective-permute-start(f32[256,8,128]{2,0,1:T(8,128)} %fusion.53), channel_id=1, source_target_pairs={{28,0},{0,4},{4,8},{8,12},{12,16},{16,20},{20,24},{24,28},{29,1},{... | collective-permute-start | bytes 3145736 | tf_op jit(solution)/shard_map/while/body/eval_jaxpr/ppermute | solution.py:13
  489.6 35.2 %collective-permute-start.4 = (f32[256,8,128]{2,0,1:T(8,128)}, f32[256,8,128]{2,0,1:T(8,128)}, u32[]{:S(2)}, u32[]{:S(2)}) collective-permute-start(f32[256,8,128]{2,0,1:T(8,128)} %fusion.54), channel_id=1, source_target_pairs={{28,0},{0,4},{4,8},{8,12},{12,16},{16,20},{20,24},{24,28},{29,1},{... | collective-permute-start | bytes 3145736 | tf_op jit(solution)/shard_map/while/body/eval_jaxpr/ppermute | solution.py:13
  489.6 35.2 %collective-permute-start = (bf16[256,8,128]{2,0,1:T(8,128)(2,1)S(1)}, bf16[256,8,128]{2,0,1:T(8,128)(2,1)}, u32[]{:S(2)}, u32[]{:S(2)}) collective-permute-start(bf16[256,8,128]{2,0,1:T(8,128)(2,1)S(1)} %copy.77), channel_id=1, source_target_pairs={{28,0},{0,4},{4,8},{8,12},{12,16},{16,20},{20,24},{24,28},{29,1},{... | collective-permute-start | bytes 1572872 | tf_op jit(solution)/shard_map/while/body/eval_jaxpr/ppermute | solution.py:13
  531.0 37.9 %collective-permute-start.3 = (f32[256,8,128]{2,0,1:T(8,128)}, f32[256,8,128]{2,0,1:T(8,128)}, u32[]{:S(2)}, u32[]{:S(2)}) collective-permute-start(f32[256,8,128]{2,0,1:T(8,128)} %fusion.53), channel_id=1, source_target_pairs={{28,0},{0,4},{4,8},{8,12},{12,16},{16,20},{20,24},{24,28},{29,1},{... | collective-permute-start | bytes 3145736 | tf_op jit(solution)/shard_map/while/body/eval_jaxpr/ppermute | solution.py:13
  533.7 35.2 %collective-permute-start.4 = (f32[256,8,128]{2,0,1:T(8,128)}, f32[256,8,128]{2,0,1:T(8,128)}, u32[]{:S(2)}, u32[]{:S(2)}) collective-permute-start(f32[256,8,128]{2,0,1:T(8,128)} %fusion.54), channel_id=1, source_target_pairs={{28,0},{0,4},{4,8},{8,12},{12,16},{16,20},{20,24},{24,28},{29,1},{... | collective-permute-start | bytes 3145736 | tf_op jit(solution)/shard_map/while/body/eval_jaxpr/ppermute | solution.py:13
  533.7 35.2 %collective-permute-start = (bf16[256,8,128]{2,0,1:T(8,128)(2,1)S(1)}, bf16[256,8,128]{2,0,1:T(8,128)(2,1)}, u32[]{:S(2)}, u32[]{:S(2)}) collective-permute-start(bf16[256,8,128]{2,0,1:T(8,128)(2,1)S(1)} %copy.77), channel_id=1, source_target_pairs={{28,0},{0,4},{4,8},{8,12},{12,16},{16,20},{20,24},{24,28},{29,1},{... | collective-permute-start | bytes 1572872 | tf_op jit(solution)/shard_map/while/body/eval_jaxpr/ppermute | solution.py:13
  575.1 37.9 %collective-permute-start.3 = (f32[256,8,128]{2,0,1:T(8,128)}, f32[256,8,128]{2,0,1:T(8,128)}, u32[]{:S(2)}, u32[]{:S(2)}) collective-permute-start(f32[256,8,128]{2,0,1:T(8,128)} %fusion.53), channel_id=1, source_target_pairs={{28,0},{0,4},{4,8},{8,12},{12,16},{16,20},{20,24},{24,28},{29,1},{... | collective-permute-start | bytes 3145736 | tf_op jit(solution)/shard_map/while/body/eval_jaxpr/ppermute | solution.py:13
  577.8 35.2 %collective-permute-start.4 = (f32[256,8,128]{2,0,1:T(8,128)}, f32[256,8,128]{2,0,1:T(8,128)}, u32[]{:S(2)}, u32[]{:S(2)}) collective-permute-start(f32[256,8,128]{2,0,1:T(8,128)} %fusion.54), channel_id=1, source_target_pairs={{28,0},{0,4},{4,8},{8,12},{12,16},{16,20},{20,24},{24,28},{29,1},{... | collective-permute-start | bytes 3145736 | tf_op jit(solution)/shard_map/while/body/eval_jaxpr/ppermute | solution.py:13
  577.8 35.2 %collective-permute-start = (bf16[256,8,128]{2,0,1:T(8,128)(2,1)S(1)}, bf16[256,8,128]{2,0,1:T(8,128)(2,1)}, u32[]{:S(2)}, u32[]{:S(2)}) collective-permute-start(bf16[256,8,128]{2,0,1:T(8,128)(2,1)S(1)} %copy.77), channel_id=1, source_target_pairs={{28,0},{0,4},{4,8},{8,12},{12,16},{16,20},{20,24},{24,28},{29,1},{... | collective-permute-start | bytes 1572872 | tf_op jit(solution)/shard_map/while/body/eval_jaxpr/ppermute | solution.py:13
  (29 other events, 667.4 us)
Sparse Core Ops, SparseCore 0:
  9.9 39.2 all-gather.6
  51.7 37.3 all-gather.4
  90.9 62.9 all-gather.8
  179.0 52.2 reduce-scatter.2
  235.3 169.2 reduce-scatter.4
